TPU v7x, 256 devices: a whole 4x4x8 slice. The times are simulated.
256 devices in a mesh: node: 16 (over y, x_hi, core), tm: 16 (over z, x_lo).
Axes of the slice: x: 4 (x_hi: 2, x_lo: 2; x = x_hi * 2 + x_lo), y: 4, z: 8, core: 2. Of those that a mesh axis runs over, the one named last changes fastest.
Arguments:
- observed: bfloat16 [65536, 16384], P('node', 'tm'), may hold values from 0.5 to 32
- node_factor: bfloat16 [64, 65536], P(None, ('node', 'tm')), may hold values from 0.19921875 to 1
- time_factor: bfloat16 [64, 1024], P(None, 'tm'), may hold values from 0.19921875 to 1
- species_factor: bfloat16 [64, 16], replicated, may hold values from 0.19921875 to 1
Outputs:
- grad_node: float32 [64, 65536], P(None, ('node', 'tm'))
- grad_time: float32 [64, 1024], P(None, 'tm')
- grad_species: float32 [64, 16], replicated
All inputs are finite; a program needn't handle non-finite values.
Results may differ from a plain program's by a relative error of at most 0.0017.
Values may be sent and summed in bfloat16 or wider, within the bound.
No kernel may reach another device: no remote copies, remote signals or barrier semaphores. Data moves between devices by JAX's collectives and lax.ppermute only.
A program may use at most 64 MiB of HBM per device.

v0:
```python
import math
import jax
import jax.numpy as jnp
from jax import lax
from jax.sharding import PartitionSpec as P


def widen(values):
    return lax.optimization_barrier(values).astype(jnp.float32)


def shards(observed, node_factor, time_factor, species_factor):
    factor_rank = node_factor.shape[0]
    time_vals = time_factor.astype(jnp.float32)
    species_vals = species_factor.astype(jnp.float32)
    time_dev = time_vals.shape[1]
    species = species_vals.shape[1]
    node_rows = observed.shape[0]
    flat_width = observed.shape[1]
    khatri = (
        (time_vals[:, :, None] * species_vals[:, None, :])
        .reshape(factor_rank, flat_width)
        .astype(jnp.bfloat16)
    )
    khatri_wide = widen(khatri)
    factor_wide = lax.all_gather(node_factor, "tm", axis=1, tiled=True).astype(jnp.float32)
    modelled = lax.dot_general(
        factor_wide, khatri_wide, (((0,), (0,)), ((), ())), precision=lax.Precision.HIGHEST
    )
    derivative = ((modelled - observed.astype(jnp.float32)) / (modelled * modelled)).astype(
        jnp.bfloat16
    )
    derivative_wide = widen(derivative)
    node_part = lax.dot_general(
        khatri_wide, derivative_wide, (((1,), (1,)), ((), ())), precision=lax.Precision.HIGHEST
    )
    node_grads = node_part
    contracted = lax.dot_general(
        derivative_wide, factor_wide, (((0,), (1,)), ((), ())), precision=lax.Precision.HIGHEST
    )
    node_grads, contracted = (node_grads, contracted)
    tm_count = lax.axis_size("tm")
    steps_all = time_dev * tm_count
    nodes_all = node_rows * lax.axis_size("node")
    share_rows = node_rows // tm_count
    summed = lax.psum(node_grads, "tm")
    grad_node = lax.dynamic_slice_in_dim(summed, lax.axis_index("tm") * share_rows, share_rows, 1)
    grad_node = grad_node / math.sqrt(steps_all * species)
    by_step = contracted.reshape(time_dev, species, factor_rank)
    time_grad = jnp.einsum("tsr,rs->rt", by_step, species_vals, precision=lax.Precision.HIGHEST)
    species_grad = jnp.einsum("tsr,rt->rs", by_step, time_vals, precision=lax.Precision.HIGHEST)
    time_grad = lax.psum(time_grad, "node")
    species_grad = lax.psum(species_grad, ("node", "tm"))
    grad_time = time_grad / math.sqrt(nodes_all * species)
    grad_species = species_grad / math.sqrt(nodes_all * steps_all)
    return (grad_node, grad_time, grad_species)


def solution(mesh):
    in_specs = (P("node", "tm"), P(None, ("node", "tm")), P(None, "tm"), P())
    out_specs = (P(None, ("node", "tm")), P(None, "tm"), P())
    return jax.shard_map(shards, mesh=mesh, in_specs=in_specs, out_specs=out_specs, check_vma=False)
```

profile of v0, /device:TPU:32, one launch (start us, length us, event | category | flops | bytes accessed | tf_op | source)
XLA Modules:
  0.0 226.5 jit_solution(11420919624136938555)
XLA Ops:
  7.2 0.0 all-reduce.2.cloned.1.call-start
  7.2 0.7 convert_element_type.22
  7.9 0.8 copy.9
  8.7 0.1 multiply_convert_fusion
  8.8 36.8 %all_gather.3 = bf16[64,4096]{1,0:T(8,128)(2,1)S(1)} all-gather(bf16[64,256]{1,0:T(8,128)(2,1)} %param.5), channel_id=1, replica_groups=mesh['node'=16,'tm'=16] {'tm'}, dimensions={1}, use_global_device_ids=true | all-gather | bytes 557056 | tf_op jit(solution)/shard_map/all_gather | solution.py:26
  45.5 11.3 %copy.10 = bf16[4096,1024]{0,1:T(8,128)(2,1)} copy(bf16[4096,1024]{1,0:T(8,128)(2,1)} %param.4) | data formatting | bytes 16777216 | tf_op args[0]
  56.8 5.7 %fusion.1 = bf16[4096,1024]{0,1:T(8,128)(2,1)S(1)} fusion(bf16[4096,1024]{0,1:T(8,128)(2,1)} %copy.10, bf16[64,1024]{0,1:T(8,128)(2,1)S(1)} %bitcast.23, bf16[64,4096]{1,0:T(8,128)(2,1)S(1)} %all_gather.3), kind=kOutput, calls=%fused_computation.3 | convolution fusion | flops 557842432 | bytes 17432576 | tf_op jit(solution)/shard_map/dot_general | solution.py:27
  62.5 0.0 copy-start
  62.5 3.2 %copy-done = bf16[4096,1024]{0,1:T(8,128)(2,1)} copy-done((bf16[4096,1024]{0,1:T(8,128)(2,1)}, bf16[4096,1024]{0,1:T(8,128)(2,1)S(1)}, u32[]{:S(2)}) %copy-start) | copy-done | bytes 8388632
  65.7 2.6 %fusion.2 = f32[64,4096]{1,0:T(8,128)} fusion(bf16[64,1024]{0,1:T(8,128)(2,1)S(1)} %bitcast.24, bf16[4096,1024]{0,1:T(8,128)(2,1)S(1)} %fusion.1), kind=kOutput, calls=%fused_computation.10 | convolution fusion | flops 536870912 | bytes 9568256 | tf_op jit(solution)/shard_map/dot_general | solution.py:34
  68.3 0.0 all-reduce.2.cloned.1.call-update
  68.3 5.7 %multiply_reduce_fusion.1 = (f32[64,64]{0,1:T(8,128)S(1)}, f32[1024,64]{1,0:T(8,128)S(1)}) fusion(f32[64,16]{0,1:T(8,128)S(1)} %convert_element_type.22, bf16[4096,1024]{0,1:T(8,128)(2,1)} %copy-done, bf16[64,4096]{1,0:T(8,128)(2,1)S(1)} %all_gather.3), kind=kOutput, calls=%fused_computation.5 | convolution fusion | flops 536997888 | bytes 9195520 | tf_op jit(solution)/shard_map/dot_general | solution.py:38
  74.0 0.1 copy.18
  74.1 0.1 multiply_reduce_fusion
  74.2 76.9 %psum.23 = f32[64,16]{0,1:T(8,128)S(1)} all-reduce(f32[64,16]{0,1:T(8,128)S(1)} %multiply_reduce_fusion), channel_id=1, replica_groups=mesh['node'=16,'tm'=16] {'node','tm'}, use_global_device_ids=true, to_apply=%region_2.0 | all-reduce | flops 1024 | bytes 8192 | tf_op jit(solution)/shard_map/psum | solution.py:53
  151.1 65.8 %psum.22 = f32[64,64]{1,0:T(8,128)S(1)} all-reduce(f32[64,64]{1,0:T(8,128)S(1)} %copy.18), channel_id=1, replica_groups=mesh['node'=16,'tm'=16] {'node'}, use_global_device_ids=true, to_apply=%region_1.0 | all-reduce | flops 4096 | bytes 32768 | tf_op jit(solution)/shard_map/psum | solution.py:52
  217.0 0.6 broadcast_multiply_fusion.1
  217.6 0.6 broadcast_multiply_fusion
  218.2 0.0 all-reduce.2.cloned.1.call-done
  218.2 1.5 dynamic-slice_multiply_fusion
Async XLA Ops:
  7.2 211.0 %all-reduce.2.cloned.1.call-start = ((), (), s32[]{:S(2)}) async-start(), calls=%async_computation | async-start | bytes 2097152 | tf_op jit(solution)/shard_map/psum | solution.py:46
  62.5 3.2 %copy-start = (bf16[4096,1024]{0,1:T(8,128)(2,1)}, bf16[4096,1024]{0,1:T(8,128)(2,1)S(1)}, u32[]{:S(2)}) copy-start(bf16[4096,1024]{0,1:T(8,128)(2,1)S(1)} %fusion.1) | copy-start | bytes 25165828
Sparse Core Ops, SparseCore 0:
  68.4 138.8 all-reduce.1
where the time goes:
time: 227 us; the launch traced here: 226 us
  blocking collectives  180 us (79%)
  local copies, waits for them, and re-layouts  15.3 us (7%)
  between operations  14.1 us (6%)
  matrix products  14 us (6%)
  other arithmetic  3.56 us (2%)
    psum x1, blocking collectives, shards(): species_grad = lax.psum(species_grad, ('node', 'tm'))  76.9 us
    psum x1, blocking collectives, shards(): time_grad = lax.psum(time_grad, 'node')  65.8 us
    all_gather x1, blocking collectives, shards(): lax.all_gather(node_factor, 'tm', axis=1, tiled=True).astype(jnp.float32)  36.8 us
    unnamed x3, local copies, waits for them, and re-layouts  14.5 us
    dot_general x1, matrix products, shards(): lax.dot_general(derivative_wide, factor_wide, (((0,), (1,)), ((), ())), p...  5.71 us
    dot_general x1, matrix products, shards(): lax.dot_general(factor_wide, khatri_wide, (((0,), (0,)), ((), ())), preci...  5.67 us
  transfers between devices with their start and end apart: 1, of which 0 were waited for; matrix products, arithmetic and copies ran while one was open for 3% of the time, Pallas kernels for 0%

commit v1 on v0

--- a/solution.py
+++ b/solution.py
@@ -3,6 +3,10 @@
 import jax.numpy as jnp
 from jax import lax
 from jax.sharding import PartitionSpec as P
+
+
+def tell_pages(m):
+    return lax.all_gather(m, axis_name=("node", "tm")).sum(axis=0)
 
 
 def widen(values):
@@ -50,7 +54,7 @@
     time_grad = jnp.einsum("tsr,rs->rt", by_step, species_vals, precision=lax.Precision.HIGHEST)
     species_grad = jnp.einsum("tsr,rt->rs", by_step, time_vals, precision=lax.Precision.HIGHEST)
     time_grad = lax.psum(time_grad, "node")
-    species_grad = lax.psum(species_grad, ("node", "tm"))
+    species_grad = tell_pages(species_grad)
     grad_time = time_grad / math.sqrt(nodes_all * species)
     grad_species = species_grad / math.sqrt(nodes_all * steps_all)
     return (grad_node, grad_time, grad_species)

time: 227 us -> 809 us (3.56)
  waiting for transfers between devices: 0.02 us -> 652 us
  blocking collectives: 180 us -> 102 us
    all_gather x0 -> x1, waiting for transfers between devices: none -> 586 us  [tell_pages(): return lax.all_gather(m, axis_name=('node', 'tm')).sum(axis=0)]
    psum x1 -> x0, blocking collectives: 76.9 us -> none  [shards(): species_grad = lax.psum(species_grad, ('node', 'tm'))]
    psum x1, waiting for transfers between devices: 0.01 us -> 66.5 us  [shards(): summed = lax.psum(node_grads, 'tm')]
  transfers between devices with their start and end apart: 1 -> 2, of which waited for: 0 -> 2; matrix products, arithmetic and copies ran while one was open for 3% -> 1% of each run, Pallas kernels for 0% -> 0%
where the time goes in v1:
time: 809 us; the launch traced here: 805 us
  waiting for transfers between devices  652 us (81%)
  blocking collectives  102 us (13%)
  between operations  15.5 us (2%)
  local copies, waits for them, and re-layouts  15.3 us (2%)
  matrix products  13.9 us (2%)
    all_gather x1, waiting for transfers between devices, tell_pages(): return lax.all_gather(m, axis_name=('node', 'tm')).sum(axis=0)  586 us
    psum x1, waiting for transfers between devices, shards(): summed = lax.psum(node_grads, 'tm')  66.5 us
    psum x1, blocking collectives, shards(): time_grad = lax.psum(time_grad, 'node')  65.5 us
    all_gather x1, blocking collectives, shards(): lax.all_gather(node_factor, 'tm', axis=1, tiled=True).astype(jnp.float32)  36.8 us
  transfers between devices with their start and end apart: 2, of which 2 were waited for; matrix products, arithmetic and copies ran while one was open for 1% of the time, Pallas kernels for 0%

profile of v1, /device:TPU:32, one launch (start us, length us, event | category | flops | bytes accessed | tf_op | source)
XLA Modules:
  0.0 805.3 jit_solution(5320316701728149048)
XLA Ops:
  8.0 0.0 all-reduce.2.cloned.1.call-start
  8.0 0.7 convert_element_type.22
  8.7 0.8 copy.12
  9.5 0.1 multiply_convert_fusion
  9.6 36.8 %all_gather.9 = bf16[64,4096]{1,0:T(8,128)(2,1)S(1)} all-gather(bf16[64,256]{1,0:T(8,128)(2,1)} %param.5), channel_id=1, replica_groups=mesh['node'=16,'tm'=16] {'tm'}, dimensions={1}, use_global_device_ids=true | all-gather | bytes 557056 | tf_op jit(solution)/shard_map/all_gather | solution.py:30
  46.4 11.3 %copy.13 = bf16[4096,1024]{0,1:T(8,128)(2,1)} copy(bf16[4096,1024]{1,0:T(8,128)(2,1)} %param.4) | data formatting | bytes 16777216 | tf_op args[0]
  57.6 5.6 fusion.1
  63.3 0.0 copy-start
  63.3 3.2 copy-done
  66.5 2.6 fusion.2
  69.1 0.0 all-reduce.2.cloned.1.call-update
  69.1 0.0 all-gather.4.cloned.1.call-start
  69.1 5.7 multiply_reduce_fusion.1
  74.8 0.7 multiply_reduce_fusion
  75.6 0.0 all-gather.4.cloned.1.call-update
  75.6 0.1 copy.21
  75.7 65.5 %psum.15 = f32[64,64]{1,0:T(8,128)S(1)} all-reduce(f32[64,64]{1,0:T(8,128)S(1)} %copy.21), channel_id=1, replica_groups=mesh['node'=16,'tm'=16] {'node'}, use_global_device_ids=true, to_apply=%region_1.0 | all-reduce | flops 4096 | bytes 32768 | tf_op jit(solution)/shard_map/psum | solution.py:56
  141.2 0.6 broadcast_multiply_fusion
  141.8 66.5 %all-reduce.2.cloned.1.call-done = f32[64,4096]{1,0:T(8,128)} async-done(((f32[64,4096]{1,0:T(8,128)}), f32[64,4096]{1,0:T(8,128)}) %all-reduce.2.cloned.1.call-update) | async-done | bytes 1048592 | tf_op jit(solution)/shard_map/psum | solution.py:50
  208.2 1.5 dynamic-slice_multiply_fusion
  209.7 585.6 %all-gather.4.cloned.1.call-done = f32[256,64,16]{1,2,0:T(8,128)} async-done(((f32[1,64,16]{1,2,0:T(8,128)}), f32[256,64,16]{1,2,0:T(8,128)}) %all-gather.4.cloned.1.call-update) | async-done | bytes 1048592 | tf_op jit(solution)/shard_map/all_gather | solution.py:9
  795.3 1.9 reduce_sum.9
  797.2 0.6 broadcast_multiply_fusion.1
Async XLA Ops:
  8.0 200.3 %all-reduce.2.cloned.1.call-start = ((), (), s32[]{:S(2)}) async-start(), calls=%async_computation | async-start | bytes 2097152 | tf_op jit(solution)/shard_map/psum | solution.py:50
  63.3 3.2 copy-start
  69.1 726.3 %all-gather.4.cloned.1.call-start = ((), (), s32[]{:S(2)}) async-start(), calls=%async_computation.1 | async-start | bytes 2105344 | tf_op jit(solution)/shard_map/all_gather | solution.py:9
Sparse Core Ops, SparseCore 0:
  69.2 138.9 all-reduce.1
Sparse Core Ops, SparseCore 1:
  75.7 719.6 all-gather.3
